TPU v7x, 512 devices: a whole 4x4x16 slice. The times are simulated.
512 devices in a mesh: req: 128 (over y, z, core), tp: 4 (over x).
Axes of the slice: x: 4, y: 4, z: 16, core: 2. Of those that a mesh axis runs over, the one named last changes fastest.
Arguments:
- tokens: bfloat16 [131072, 3584], P('req', 'tp'), may hold values from -6 to 6
- key_value_weight: bfloat16 [3584, 1024], P('tp'), may hold values from -0.09375 to 0.09375
- adapter_down_maps: bfloat16 [128, 16, 3584], P('req', None, 'tp'), may hold values from -0.09375 to 0.09375
- adapter_up_maps: bfloat16 [128, 16, 1024], P('req', None, 'tp'), may hold values from -1.5 to 1.5
- block_adapter_ids: int32 [1024], P('req'), may hold values from 0 to 127, never falling along the last dimension, each value on 1 to 32 neighbouring positions
- block_live_rows: int32 [1024], P('req'), may hold values from 32 to 128
- adapter_storage_slot: int32 [128], replicated, may hold values from 0 to 127, each once
Outputs:
- keys_values: bfloat16 [131072, 1024], P('req', 'tp')
Inputs may be any that keep to these rules, and one draw needn't show every extreme that they name: `block_adapter_ids`: block ids never fall from one block to the next, every adapter id names at least one block, and one adapter names 32 blocks. `adapter_storage_slot`: each storage slot belongs to exactly one adapter.
All inputs are finite; a program needn't handle non-finite values.
Results may differ from a plain program's by a relative error of at most 0.003.
Values may be sent and summed in bfloat16 or wider, within the bound.
No kernel may reach another device: no remote copies, remote signals or barrier semaphores. Data moves between devices by JAX's collectives and lax.ppermute only.
A program may use at most 64 MiB of HBM per device.

v0:
```python
import jax
import jax.numpy as jnp
from jax import lax
from jax.sharding import PartitionSpec as P

adapter_scale = 0.5


def shards(
    tokens,
    key_value_weight,
    adapter_down_maps,
    adapter_up_maps,
    block_adapter_ids,
    block_live_rows,
    adapter_storage_slot,
):
    rows_dev, width_dev = tokens.shape
    blocks_dev = block_adapter_ids.shape[0]
    block_rows = rows_dev // blocks_dev
    local_columns = adapter_up_maps.shape[2]
    adapter_count = adapter_storage_slot.shape[0]
    matches = (
        block_adapter_ids[:, None] == jnp.arange(adapter_count, dtype=jnp.int32)[None, :]
    ).astype(jnp.int32)
    slot_ids = jnp.sum(matches * adapter_storage_slot[None, :], axis=1)
    pieces = (
        lax.all_gather(adapter_down_maps, "req", axis=0, tiled=True),
        lax.all_gather(adapter_up_maps, "req", axis=0, tiled=True),
    )
    piece_count = pieces[0].shape[0]
    chosen = (slot_ids[:, None] == jnp.arange(piece_count, dtype=jnp.int32)[None, :]).astype(
        jnp.bfloat16
    )
    a_part = jnp.einsum("bj,jrd->brd", chosen, pieces[0], preferred_element_type=jnp.float32)
    b_part = jnp.einsum("bj,jrc->brc", chosen, pieces[1], preferred_element_type=jnp.float32)
    chosen_down_maps = a_part.astype(jnp.bfloat16)
    chosen_up_maps = b_part.astype(jnp.bfloat16)
    features_all = lax.all_gather(tokens, "tp", axis=1, tiled=True)
    tp_index = lax.axis_index("tp")
    own_part = lax.dynamic_slice_in_dim(
        lax.all_gather(key_value_weight, "tp", axis=0, tiled=True),
        tp_index * local_columns,
        local_columns,
        1,
    )
    base_result = jnp.dot(features_all, own_part, preferred_element_type=jnp.float32)
    complete_down_maps = lax.all_gather(chosen_down_maps, "tp", axis=2, tiled=True)
    blocked_input = features_all.reshape(blocks_dev, block_rows, features_all.shape[1])
    rank_reduced = jnp.einsum(
        "qzo,qjo->qzj", blocked_input, complete_down_maps, preferred_element_type=jnp.float32
    )
    low_values = rank_reduced.astype(jnp.bfloat16)
    adapter_result = jnp.einsum(
        "bkr,brc->bkc", low_values, chosen_up_maps, preferred_element_type=jnp.float32
    ).reshape(rows_dev, local_columns)
    live_rows = (
        jnp.arange(block_rows, dtype=jnp.int32)[None, :] < block_live_rows[:, None]
    ).reshape(rows_dev, 1)
    adapted_output = base_result + adapter_scale * adapter_result
    return jnp.where(live_rows, adapted_output, jnp.zeros_like(adapted_output)).astype(jnp.bfloat16)


def solution(mesh):
    in_specs = (
        P("req", "tp"),
        P("tp", None),
        P("req", None, "tp"),
        P("req", None, "tp"),
        P("req"),
        P("req"),
        P(),
    )
    out_specs = P("req", "tp")
    return jax.shard_map(shards, mesh=mesh, in_specs=in_specs, out_specs=out_specs, check_vma=False)
```

profile of v0, /device:TPU:1, one launch (start us, length us, event | category | flops | bytes accessed | tf_op | source)
XLA Modules:
  0.0 465.4 jit_solution(3460865263811185851)
XLA Ops:
  6.5 0.0 all-gather.11.cloned.1.call-start
  6.5 0.7 all-gather.11.cloned.1.call-update
  7.3 0.0 all-gather.9.cloned.1.call-start
  7.3 0.7 all-gather.9.cloned.1.call-update
  8.0 0.0 all-gather.7.cloned.1.call-start
  8.1 0.7 all-gather.7.cloned.1.call-update
  8.7 0.0 all-gather.5.cloned.1.call-start
  8.8 0.5 all-gather.5.cloned.1.call-update
  9.3 0.9 select_reduce_fusion
  10.2 0.7 fusion.23
  10.9 136.2 %all-gather.11.cloned.1.call-done = bf16[128,16,256]{2,1,0:T(8,128)(2,1)} async-done(((bf16[1,16,256]{2,1,0:T(8,128)(2,1)}), bf16[128,16,256]{2,1,0:T(8,128)(2,1)}) %all-gather.11.cloned.1.call-update) | async-done | bytes 1048592 | tf_op jit(solution)/shard_map/all_gather | solution.py:29
  147.1 1.6 convolution_convert_fusion
  148.7 139.3 %all-gather.9.cloned.1.call-done = bf16[128,16,896]{2,1,0:T(8,128)(2,1)} async-done(((bf16[1,16,896]{2,1,0:T(8,128)(2,1)}), bf16[128,16,896]{2,1,0:T(8,128)(2,1)}) %all-gather.9.cloned.1.call-update) | async-done | bytes 3670032 | tf_op jit(solution)/shard_map/all_gather | solution.py:28
  287.9 3.0 fusion.16
  291.0 12.6 %all_gather.18 = bf16[8,16,3584]{2,0,1:T(8,128)(2,1)S(1)} all-gather(bf16[8,16,896]{2,0,1:T(8,128)(2,1)S(1)} %fusion.16), channel_id=1, replica_groups=mesh['req'=128,'tp'=4] {'tp'}, dimensions={2}, use_global_device_ids=true | all-gather | bytes 1146880 | tf_op jit(solution)/shard_map/all_gather | solution.py:48
  303.5 63.6 %all-gather.7.cloned.1.call-done = bf16[1024,3584]{1,0:T(8,128)(2,1)} async-done(((bf16[1024,896]{1,0:T(8,128)(2,1)}), bf16[1024,3584]{1,0:T(8,128)(2,1)}) %all-gather.7.cloned.1.call-update) | async-done | bytes 7340048 | tf_op jit(solution)/shard_map/all_gather | solution.py:39
  367.2 5.3 %convolution_multiply_fusion = f32[8,128,256]{2,1,0:T(8,128)S(1)} fusion(bf16[8,128,3584]{2,1,0:T(8,128)(2,1)} %bitcast.18, bf16[8,16,3584]{2,0,1:T(8,128)(2,1)S(1)} %all_gather.18, bf16[8,16,256]{2,0,1:T(8,128)(2,1)S(1)} %convolution_convert_fusion), kind=kOutput, calls=%fused_computation.5 | convolution fusion | flops 126107648 | bytes 9371648 | tf_op jit(solution)/shard_map/bkr,brc->bkc/dot_general | solution.py:54
  372.5 0.3 copy.18
  372.8 79.2 %all-gather.5.cloned.1.call-done = bf16[3584,1024]{1,0:T(8,128)(2,1)} async-done(((bf16[896,1024]{1,0:T(8,128)(2,1)}), bf16[3584,1024]{1,0:T(8,128)(2,1)}) %all-gather.5.cloned.1.call-update) | async-done | bytes 7340048 | tf_op jit(solution)/shard_map/all_gather | solution.py:42
  452.0 5.8 %fusion.13 = bf16[1024,256]{0,1:T(8,128)(2,1)S(1)} fusion(f32[1024,256]{0,1:T(8,128)S(1)} %copy.18, bf16[1024,3584]{1,0:T(8,128)(2,1)} %all-gather.7.cloned.1.call-done, bf16[3584,1024]{1,0:T(8,128)(2,1)} %all-gather.5.cloned.1.call-done, s32[]{:T(128)S(6)} %select_n.7, pred[1024]{0:T(1024)(128)(4,1)S(1)} %fusion.23), kind=kOutput, calls=%fused_computation.8 | convolution fusion | flops 1879834624 | bytes 10748932 | tf_op jit(solution)/shard_map/dot_general | solution.py:47
  457.8 1.0 copy.17
Async XLA Ops:
  6.5 140.5 %all-gather.11.cloned.1.call-start = ((), (), s32[]{:S(2)}) async-start(), calls=%async_computation.3 | async-start | bytes 1056768 | tf_op jit(solution)/shard_map/all_gather | solution.py:29
  7.3 280.7 %all-gather.9.cloned.1.call-start = ((), (), s32[]{:S(2)}) async-start(), calls=%async_computation.2 | async-start | bytes 3698688 | tf_op jit(solution)/shard_map/all_gather | solution.py:28
  8.0 359.1 %all-gather.7.cloned.1.call-start = ((), (), s32[]{:S(2)}) async-start(), calls=%async_computation.1 | async-start | bytes 9175040 | tf_op jit(solution)/shard_map/all_gather | solution.py:39
  8.7 443.3 %all-gather.5.cloned.1.call-start = ((), (), s32[]{:S(2)}) async-start(), calls=%async_computation | async-start | bytes 9175040 | tf_op jit(solution)/shard_map/all_gather | solution.py:42
Sparse Core Ops, SparseCore 0:
  10.3 136.7 all-gather.10
  150.1 137.7 all-gather.8
  290.1 77.0 all-gather.6
  369.1 82.8 all-gather.4
where the time goes:
time: 466 us; the launch traced here: 465 us
  waiting for transfers between devices  421 us (90%)
  matrix products  15.7 us (3%)
  between operations  13.2 us (3%)
  blocking collectives  12.6 us (3%)
    all_gather x1, waiting for transfers between devices, shards(): lax.all_gather(adapter_down_maps, 'req', axis=0, tiled=True)  139 us
    all_gather x1, waiting for transfers between devices, shards(): lax.all_gather(adapter_up_maps, 'req', axis=0, tiled=True)  136 us
    all_gather x1, waiting for transfers between devices, shards(): lax.all_gather(key_value_weight, 'tp', axis=0, tiled=True)  79.2 us
    all_gather x1, waiting for transfers between devices, shards(): features_all = lax.all_gather(tokens, 'tp', axis=1, tiled=True)  63.6 us
    all_gather x1, blocking collectives, shards(): lax.all_gather(chosen_down_maps, 'tp', axis=2, tiled=True)  12.6 us
  transfers between devices with their start and end apart: 4, of which 4 were waited for; matrix products, arithmetic and copies ran while one was open for 3% of the time, Pallas kernels for 0%

commit v1 on v0

--- a/solution.py
+++ b/solution.py
@@ -24,9 +24,18 @@
         block_adapter_ids[:, None] == jnp.arange(adapter_count, dtype=jnp.int32)[None, :]
     ).astype(jnp.int32)
     slot_ids = jnp.sum(matches * adapter_storage_slot[None, :], axis=1)
+    answer_matrix_by_axis = lambda my_data: jnp.concatenate(
+        lax.all_to_all(
+            jnp.stack(lax.axis_size("req") * [my_data], axis=0),
+            axis_name="req",
+            split_axis=0,
+            concat_axis=0,
+        ),
+        axis=0,
+    )
     pieces = (
         lax.all_gather(adapter_down_maps, "req", axis=0, tiled=True),
-        lax.all_gather(adapter_up_maps, "req", axis=0, tiled=True),
+        answer_matrix_by_axis(adapter_up_maps),
     )
     piece_count = pieces[0].shape[0]
     chosen = (slot_ids[:, None] == jnp.arange(piece_count, dtype=jnp.int32)[None, :]).astype(

time: 466 us -> 339 us (0.73)
  waiting for transfers between devices: 421 us -> 273 us
  starting transfers between devices: 0.12 us -> 20.6 us
    all_gather x1 -> x0, waiting for transfers between devices: 136 us -> none  [shards(): lax.all_gather(adapter_up_maps, 'req', axis=0, tiled=True)]
    all_gather x1, waiting for transfers between devices: 139 us -> 73.3 us  [shards(): lax.all_gather(adapter_down_maps, 'req', axis=0, tiled=True)]
    all_to_all x0 -> x1, waiting for transfers between devices: none -> 55 us  [shards(): lax.all_to_all(jnp.stack(lax.axis_size('req') * [my_data], axis=0), axis_...]
    all_to_all x0 -> x1, starting transfers between devices: none -> 20.6 us  [shards(): lax.all_to_all(jnp.stack(lax.axis_size('req') * [my_data], axis=0), axis_...]
  transfers between devices with their start and end apart: 4 -> 4, of which waited for: 4 -> 4; matrix products, arithmetic and copies ran while one was open for 3% -> 4% of each run, Pallas kernels for 0% -> 0%
where the time goes in v1:
time: 339 us
  waiting for transfers between devices  273 us (81%)
  starting transfers between devices  20.6 us (6%)
  matrix products  14.5 us (4%)
  between operations  13.1 us (4%)
  blocking collectives  12.6 us (4%)
    all_gather x1, waiting for transfers between devices, shards(): lax.all_gather(key_value_weight, 'tp', axis=0, tiled=True)  79.4 us
    all_gather x1, waiting for transfers between devices, shards(): lax.all_gather(adapter_down_maps, 'req', axis=0, tiled=True)  73.3 us
    all_gather x1, waiting for transfers between devices, shards(): features_all = lax.all_gather(tokens, 'tp', axis=1, tiled=True)  63.6 us
    all_to_all x1, waiting for transfers between devices, shards(): lax.all_to_all(jnp.stack(lax.axis_size('req') * [my_data], axis=0), axis_...  55 us
    all_to_all x1, starting transfers between devices, shards(): lax.all_to_all(jnp.stack(lax.axis_size('req') * [my_data], axis=0), axis_...  20.6 us
    all_gather x1, blocking collectives, shards(): lax.all_gather(chosen_down_maps, 'tp', axis=2, tiled=True)  12.6 us
  transfers between devices with their start and end apart: 4, of which 4 were waited for; matrix products, arithmetic and copies ran while one was open for 4% of the time, Pallas kernels for 0%

profile of v1, /device:TPU:1, one launch (start us, length us, event | category | flops | bytes accessed | tf_op | source)
XLA Modules:
  0.0 338.8 jit_solution(14111409945763071766)
XLA Ops:
  6.5 0.0 all-gather.8.cloned.1.call-start
  6.5 0.7 all-gather.8.cloned.1.call-update
  7.3 0.0 all-gather.6.cloned.1.call-start
  7.3 0.7 all-gather.6.cloned.1.call-update
  8.0 0.0 all-gather.4.cloned.1.call-start
  8.1 0.7 all-gather.4.cloned.1.call-update
  8.7 1.7 stack.2
  10.5 20.6 %all-to-all-start = ((bf16[128,1,16,256]{3,2,1,0:T(8,128)(2,1)}), bf16[128,1,16,256]{3,2,1,0:T(8,128)(2,1)S(1)}, u32[]{:S(2)}, u32[]{:S(2)}) async-start(bf16[128,1,16,256]{3,2,1,0:T(8,128)(2,1)} %stack.2), calls=%async_computation | async-start | bytes 2097152 | tf_op jit(solution)/shard_map/all_to_all | solution.py:28
  31.0 0.9 select_reduce_fusion
  31.9 0.7 fusion.24
  32.6 55.0 %all-to-all-done = bf16[128,1,16,256]{3,2,1,0:T(8,128)(2,1)S(1)} async-done(((bf16[128,1,16,256]{3,2,1,0:T(8,128)(2,1)}), bf16[128,1,16,256]{3,2,1,0:T(8,128)(2,1)S(1)}, u32[]{:S(2)}, u32[]{:S(2)}) %all-to-all-start) | async-done | bytes 1048608 | tf_op jit(solution)/shard_map/all_to_all | solution.py:28
  87.6 0.4 convolution_convert_fusion
  88.0 73.3 %all-gather.8.cloned.1.call-done = bf16[128,16,896]{2,1,0:T(8,128)(2,1)} async-done(((bf16[1,16,896]{2,1,0:T(8,128)(2,1)}), bf16[128,16,896]{2,1,0:T(8,128)(2,1)}) %all-gather.8.cloned.1.call-update) | async-done | bytes 3670032 | tf_op jit(solution)/shard_map/all_gather | solution.py:37
  161.3 3.0 fusion.16
  164.3 12.6 %all_gather.15 = bf16[8,16,3584]{2,0,1:T(8,128)(2,1)S(1)} all-gather(bf16[8,16,896]{2,0,1:T(8,128)(2,1)S(1)} %fusion.16), channel_id=1, replica_groups=mesh['req'=128,'tp'=4] {'tp'}, dimensions={2}, use_global_device_ids=true | all-gather | bytes 1146880 | tf_op jit(solution)/shard_map/all_gather | solution.py:57
  176.9 63.6 %all-gather.6.cloned.1.call-done = bf16[1024,3584]{1,0:T(8,128)(2,1)} async-done(((bf16[1024,896]{1,0:T(8,128)(2,1)}), bf16[1024,3584]{1,0:T(8,128)(2,1)}) %all-gather.6.cloned.1.call-update) | async-done | bytes 7340048 | tf_op jit(solution)/shard_map/all_gather | solution.py:48
  240.5 5.3 %convolution_multiply_fusion = f32[8,128,256]{2,1,0:T(8,128)S(1)} fusion(bf16[8,128,3584]{2,1,0:T(8,128)(2,1)} %bitcast.22, bf16[8,16,3584]{2,0,1:T(8,128)(2,1)S(1)} %all_gather.15, bf16[8,16,256]{2,0,1:T(8,128)(2,1)S(1)} %convolution_convert_fusion), kind=kOutput, calls=%fused_computation.5 | convolution fusion | flops 126107648 | bytes 9371648 | tf_op jit(solution)/shard_map/bkr,brc->bkc/dot_general | solution.py:63
  245.8 0.3 copy.23
  246.2 79.4 %all-gather.4.cloned.1.call-done = bf16[3584,1024]{1,0:T(8,128)(2,1)} async-done(((bf16[896,1024]{1,0:T(8,128)(2,1)}), bf16[3584,1024]{1,0:T(8,128)(2,1)}) %all-gather.4.cloned.1.call-update) | async-done | bytes 7340048 | tf_op jit(solution)/shard_map/all_gather | solution.py:51
  325.5 5.8 %fusion.13 = bf16[1024,256]{0,1:T(8,128)(2,1)S(1)} fusion(f32[1024,256]{0,1:T(8,128)S(1)} %copy.23, bf16[1024,3584]{1,0:T(8,128)(2,1)} %all-gather.6.cloned.1.call-done, bf16[3584,1024]{1,0:T(8,128)(2,1)} %all-gather.4.cloned.1.call-done, s32[]{:T(128)S(6)} %select_n.7, pred[1024]{0:T(1024)(128)(4,1)S(1)} %fusion.24), kind=kOutput, calls=%fused_computation.8 | convolution fusion | flops 1879834624 | bytes 10748932 | tf_op jit(solution)/shard_map/dot_general | solution.py:56
  331.3 1.0 copy.22
Async XLA Ops:
  6.5 154.7 %all-gather.8.cloned.1.call-start = ((), (), s32[]{:S(2)}) async-start(), calls=%async_computation.3 | async-start | bytes 3698688 | tf_op jit(solution)/shard_map/all_gather | solution.py:37
  7.3 233.2 %all-gather.6.cloned.1.call-start = ((), (), s32[]{:S(2)}) async-start(), calls=%async_computation.2 | async-start | bytes 9175040 | tf_op jit(solution)/shard_map/all_gather | solution.py:48
  8.0 317.5 %all-gather.4.cloned.1.call-start = ((), (), s32[]{:S(2)}) async-start(), calls=%async_computation.1 | async-start | bytes 9175040 | tf_op jit(solution)/shard_map/all_gather | solution.py:51
  10.5 77.1 %all-to-all-start = ((bf16[128,1,16,256]{3,2,1,0:T(8,128)(2,1)}), bf16[128,1,16,256]{3,2,1,0:T(8,128)(2,1)S(1)}, u32[]{:S(2)}, u32[]{:S(2)}) async-start(bf16[128,1,16,256]{3,2,1,0:T(8,128)(2,1)} %stack.2), calls=%async_computation | async-start | bytes 2097152 | tf_op jit(solution)/shard_map/all_to_all | solution.py:28
Sparse Core Ops, SparseCore 0:
  10.4 150.8 all-gather.7
  163.4 77.0 all-gather.5
  242.6 82.8 all-gather.3

commit v2 on v0

--- a/solution.py
+++ b/solution.py
@@ -15,6 +15,33 @@
     block_live_rows,
     adapter_storage_slot,
 ):
+
+    def drive_pools(packet, shard_axis):
+        before = lax.axis_index(shard_axis)
+        arr_out = lax.axis_size(shard_axis)
+        piece_next, heard, q_next = (arr_out, before, packet.shape[0])
+        chunks = [num * piece_next if u == 0 else num for u, num in enumerate(packet.shape)]
+        odd = jnp.zeros(chunks, packet.dtype)
+        fresh = far_arr = packet
+        reply = lax.dynamic_update_slice_in_dim(odd, packet, heard * q_next, axis=0)
+        for h in [*range(1, piece_next // 2 + 1)]:
+            fresh = lax.ppermute(
+                fresh, shard_axis, perm=[(u, (u + 1) % piece_next) for u in range(piece_next)]
+            )
+            reply = lax.dynamic_update_slice_in_dim(
+                reply, fresh, (heard - h) % piece_next * q_next, axis=0
+            )
+            if 2 * h < piece_next:
+                far_arr = lax.ppermute(
+                    far_arr,
+                    axis_name=shard_axis,
+                    perm=[(u, (u - 1) % piece_next) for u in range(piece_next)],
+                )
+                reply = lax.dynamic_update_slice_in_dim(
+                    reply, far_arr, (heard + h) % piece_next * q_next, axis=0
+                )
+        return reply
+
     rows_dev, width_dev = tokens.shape
     blocks_dev = block_adapter_ids.shape[0]
     block_rows = rows_dev // blocks_dev
@@ -39,10 +66,7 @@
     features_all = lax.all_gather(tokens, "tp", axis=1, tiled=True)
     tp_index = lax.axis_index("tp")
     own_part = lax.dynamic_slice_in_dim(
-        lax.all_gather(key_value_weight, "tp", axis=0, tiled=True),
-        tp_index * local_columns,
-        local_columns,
-        1,
+        drive_pools(key_value_weight, "tp"), tp_index * local_columns, local_columns, 1
     )
     base_result = jnp.dot(features_all, own_part, preferred_element_type=jnp.float32)
     complete_down_maps = lax.all_gather(chosen_down_maps, "tp", axis=2, tiled=True)

time: 466 us -> 387 us (0.83)
  waiting for transfers between devices: 421 us -> 315 us
  local copies, waits for them, and re-layouts: 1.33 us -> 15.4 us
  starting transfers between devices: 0.12 us -> 13.8 us
    all_gather x1 -> x0, waiting for transfers between devices: 79.2 us -> none  [shards(): lax.all_gather(key_value_weight, 'tp', axis=0, tiled=True)]
    all_gather x1, waiting for transfers between devices: 136 us -> 80.2 us  [shards(): lax.all_gather(adapter_up_maps, 'req', axis=0, tiled=True)]
    ppermute x0 -> x3, waiting for transfers between devices: none -> 32.3 us  [the longest x2 32.3 us: drive_pools(): lax.ppermute(fresh, shard_axis, perm=[(u, (u + 1) % piece_next) for u in...]
    ppermute x0 -> x3, starting transfers between devices: none -> 13.8 us  [the longest x2 10.6 us: drive_pools(): lax.ppermute(fresh, shard_axis, perm=[(u, (u + 1) % piece_next) for u in...]
    dynamic_update_slice x0 -> x4, local copies, waits for them, and re-layouts: none -> 10.1 us  [the longest x2 5.78 us: drive_pools(): lax.dynamic_update_slice_in_dim(reply, fresh, (heard - h) % piece_next *...]
  transfers between devices with their start and end apart: 4 -> 6, of which waited for: 4 -> 4; matrix products, arithmetic and copies ran while one was open for 3% -> 5% of each run, Pallas kernels for 0% -> 0%
where the time goes in v2:
time: 387 us; the launch traced here: 386 us
  waiting for transfers between devices  315 us (81%)
  matrix products  15.8 us (4%)
  local copies, waits for them, and re-layouts  15.4 us (4%)
  starting transfers between devices  13.8 us (4%)
  between operations  13.2 us (3%)
  blocking collectives  12.6 us (3%)
    all_gather x1, waiting for transfers between devices, shards(): lax.all_gather(adapter_down_maps, 'req', axis=0, tiled=True)  136 us
    all_gather x1, waiting for transfers between devices, shards(): lax.all_gather(adapter_up_maps, 'req', axis=0, tiled=True)  80.2 us
    all_gather x1, waiting for transfers between devices, shards(): features_all = lax.all_gather(tokens, 'tp', axis=1, tiled=True)  63.6 us
    ppermute x2, waiting for transfers between devices, drive_pools(): lax.ppermute(fresh, shard_axis, perm=[(u, (u + 1) % piece_next) for u in...  32.3 us
    all_gather x1, blocking collectives, shards(): lax.all_gather(chosen_down_maps, 'tp', axis=2, tiled=True)  12.6 us
    ppermute x2, starting transfers between devices, drive_pools(): lax.ppermute(fresh, shard_axis, perm=[(u, (u + 1) % piece_next) for u in...  10.6 us
  transfers between devices with their start and end apart: 6, of which 4 were waited for; matrix products, arithmetic and copies ran while one was open for 5% of the time, Pallas kernels for 0%

profile of v2, /device:TPU:1, one launch (start us, length us, event | category | flops | bytes accessed | tf_op | source)
XLA Modules:
  0.0 386.2 jit_solution(13510352539915977908)
XLA Ops:
  6.5 0.7 all-gather.8.cloned.1.call-update
  7.3 0.7 all-gather.6.cloned.1.call-update
  8.1 0.7 all-gather.4.cloned.1.call-update
  8.7 3.9 %collective-permute-start = (bf16[896,1024]{1,0:T(8,128)(2,1)}, bf16[896,1024]{1,0:T(8,128)(2,1)}, u32[]{:S(2)}, u32[]{:S(2)}) collective-permute-start(bf16[896,1024]{1,0:T(8,128)(2,1)} %param.8), channel_id=1, source_target_pairs={{0,1},{1,2},{2,3},{3,0},{4,5},{5,6},{6,7},{7,4},{8,9},{9,10},{10,1... | collective-permute-start | bytes 5505032 | tf_op jit(solution)/shard_map/ppermute | solution.py:28
  12.7 3.2 collective-permute-start.1
  15.9 32.3 %collective-permute-done = bf16[896,1024]{1,0:T(8,128)(2,1)} collective-permute-done((bf16[896,1024]{1,0:T(8,128)(2,1)}, bf16[896,1024]{1,0:T(8,128)(2,1)}, u32[]{:S(2)}, u32[]{:S(2)}) %collective-permute-start) | collective-permute-done | bytes 1835040 | tf_op jit(solution)/shard_map/ppermute | solution.py:28
  48.2 6.6 %collective-permute-start.2 = (bf16[896,1024]{1,0:T(8,128)(2,1)}, bf16[896,1024]{1,0:T(8,128)(2,1)}, u32[]{:S(2)}, u32[]{:S(2)}) collective-permute-start(bf16[896,1024]{1,0:T(8,128)(2,1)} %collective-permute-done), channel_id=1, source_target_pairs={{0,1},{1,2},{2,3},{3,0},{4,5},{5,6},{6,7},{7,4},{8,9},{9,10},{10,1... | collective-permute-start | bytes 5505032 | tf_op jit(solution)/shard_map/ppermute | solution.py:28
  54.9 0.9 select_reduce_fusion
  55.7 3.9 %broadcast_in_dim.10 = bf16[3584,1024]{1,0:T(8,128)(2,1)} broadcast(bf16[]{:T(256)} %constant.34.clone.1), dimensions={} | broadcast | bytes 7340034 | tf_op jit(solution)/shard_map/broadcast_in_dim | solution.py:24
  59.7 1.4 constant_dynamic-update-slice_fusion.3
  61.1 0.1 fusion.23
  61.2 2.9 constant_dynamic-update-slice_fusion.2
  64.1 2.9 constant_dynamic-update-slice_fusion.1
  66.9 80.2 %all-gather.8.cloned.1.call-done = bf16[128,16,256]{2,1,0:T(8,128)(2,1)} async-done(((bf16[1,16,256]{2,1,0:T(8,128)(2,1)}), bf16[128,16,256]{2,1,0:T(8,128)(2,1)}) %all-gather.8.cloned.1.call-update) | async-done | bytes 1048592 | tf_op jit(solution)/shard_map/all_gather | solution.py:56
  147.1 1.6 convolution_convert_fusion
  148.7 2.9 constant_dynamic-update-slice_fusion
  151.6 136.4 %all-gather.6.cloned.1.call-done = bf16[128,16,896]{2,1,0:T(8,128)(2,1)} async-done(((bf16[1,16,896]{2,1,0:T(8,128)(2,1)}), bf16[128,16,896]{2,1,0:T(8,128)(2,1)}) %all-gather.6.cloned.1.call-update) | async-done | bytes 3670032 | tf_op jit(solution)/shard_map/all_gather | solution.py:55
  288.0 3.0 fusion.16
  291.0 12.6 %all_gather.14 = bf16[8,16,3584]{2,0,1:T(8,128)(2,1)S(1)} all-gather(bf16[8,16,896]{2,0,1:T(8,128)(2,1)S(1)} %fusion.16), channel_id=1, replica_groups=mesh['req'=128,'tp'=4] {'tp'}, dimensions={2}, use_global_device_ids=true | all-gather | bytes 1146880 | tf_op jit(solution)/shard_map/all_gather | solution.py:72
  303.6 63.6 %all-gather.4.cloned.1.call-done = bf16[1024,3584]{1,0:T(8,128)(2,1)} async-done(((bf16[1024,896]{1,0:T(8,128)(2,1)}), bf16[1024,3584]{1,0:T(8,128)(2,1)}) %all-gather.4.cloned.1.call-update) | async-done | bytes 7340048 | tf_op jit(solution)/shard_map/all_gather | solution.py:66
  367.2 5.3 %convolution_multiply_fusion = f32[8,128,256]{2,1,0:T(8,128)S(1)} fusion(bf16[8,128,3584]{2,1,0:T(8,128)(2,1)} %bitcast.18, bf16[8,16,3584]{2,0,1:T(8,128)(2,1)S(1)} %all_gather.14, bf16[8,16,256]{2,0,1:T(8,128)(2,1)S(1)} %convolution_convert_fusion), kind=kOutput, calls=%fused_computation.5 | convolution fusion | flops 126107648 | bytes 9371648 | tf_op jit(solution)/shard_map/bkr,brc->bkc/dot_general | solution.py:78
  372.6 0.3 copy.18
  372.9 5.8 %fusion.13 = bf16[1024,256]{0,1:T(8,128)(2,1)S(1)} fusion(f32[1024,256]{0,1:T(8,128)S(1)} %copy.18, bf16[1024,3584]{1,0:T(8,128)(2,1)} %all-gather.4.cloned.1.call-done, bf16[3584,1024]{1,0:T(8,128)(2,1)} %constant_dynamic-update-slice_fusion, s32[]{:T(128)S(6)} %select_n.41, pred[1024]{0:T(1024)(128)(4,1)S(1)} %fusion.23), kind=kOutput, calls=%fused_computation.8 | convolution fusion | flops 1879834624 | bytes 10748932 | tf_op jit(solution)/shard_map/dot_general | solution.py:71
  378.7 1.0 copy.17
  (9 shorter events, 0.1 us)
Async XLA Ops:
  6.5 53.1 %copy-start = (bf16[896,1024]{1,0:T(8,128)(2,1)S(1)}, bf16[896,1024]{1,0:T(8,128)(2,1)}, u32[]{:S(2)}) copy-start(bf16[896,1024]{1,0:T(8,128)(2,1)} %param.8) | copy-start | bytes 5505028
  6.5 54.6 %copy-start.1 = (s32[8]{0:T(128)S(1)}, s32[8]{0:T(128)}, u32[]{:S(2)}) copy-start(s32[8]{0:T(128)} %param.12) | copy-start | bytes 100
  6.5 140.6 %all-gather.8.cloned.1.call-start = ((), (), s32[]{:S(2)}) async-start(), calls=%async_computation.2 | async-start | bytes 1056768 | tf_op jit(solution)/shard_map/all_gather | solution.py:56
  7.3 280.7 %all-gather.6.cloned.1.call-start = ((), (), s32[]{:S(2)}) async-start(), calls=%async_computation.1 | async-start | bytes 3698688 | tf_op jit(solution)/shard_map/all_gather | solution.py:55
  8.0 359.2 %all-gather.4.cloned.1.call-start = ((), (), s32[]{:S(2)}) async-start(), calls=%async_computation | async-start | bytes 9175040 | tf_op jit(solution)/shard_map/all_gather | solution.py:66
  8.7 39.4 %collective-permute-start = (bf16[896,1024]{1,0:T(8,128)(2,1)}, bf16[896,1024]{1,0:T(8,128)(2,1)}, u32[]{:S(2)}, u32[]{:S(2)}) collective-permute-start(bf16[896,1024]{1,0:T(8,128)(2,1)} %param.8), channel_id=1, source_target_pairs={{0,1},{1,2},{2,3},{3,0},{4,5},{5,6},{6,7},{7,4},{8,9},{9,10},{10,1... | collective-permute-start | bytes 5505032 | tf_op jit(solution)/shard_map/ppermute | solution.py:28
  12.7 51.4 %collective-permute-start.1 = (bf16[896,1024]{1,0:T(8,128)(2,1)}, bf16[896,1024]{1,0:T(8,128)(2,1)}, u32[]{:S(2)}, u32[]{:S(2)}) collective-permute-start(bf16[896,1024]{1,0:T(8,128)(2,1)} %param.8), channel_id=1, source_target_pairs={{0,3},{1,0},{2,1},{3,2},{4,7},{5,4},{6,5},{7,6},{8,11},{9,8},{10,9... | collective-permute-start | bytes 5505032 | tf_op jit(solution)/shard_map/ppermute | solution.py:35
  48.2 100.5 %collective-permute-start.2 = (bf16[896,1024]{1,0:T(8,128)(2,1)}, bf16[896,1024]{1,0:T(8,128)(2,1)}, u32[]{:S(2)}, u32[]{:S(2)}) collective-permute-start(bf16[896,1024]{1,0:T(8,128)(2,1)} %collective-permute-done), channel_id=1, source_target_pairs={{0,1},{1,2},{2,3},{3,0},{4,5},{5,6},{6,7},{7,4},{8,9},{9,10},{10,1... | collective-permute-start | bytes 5505032 | tf_op jit(solution)/shard_map/ppermute | solution.py:28
Sparse Core Ops, SparseCore 0:
  10.3 136.7 all-gather.7
  150.1 137.8 all-gather.5
  290.1 77.0 all-gather.3
